TPU v7x, 32 devices: a whole 2x2x4 slice. The times are simulated.
32 devices in a mesh: slab: 8 (over y, x, core), view: 4 (over z).
Axes of the slice: x: 2, y: 2, z: 4, core: 2. Of those that a mesh axis runs over, the one named last changes fastest.
Arguments:
- estimate: float32 [4, 1024, 1024], P(None, 'slab'), may hold values from 0.5 to 2
- views: float32 [4, 4, 1024, 1024], P('view', None, 'slab'), may hold values from 0.25 to 4
- psf: float32 [4, 1024, 1024], P('view', 'slab'), as said below
- pattern_mult: int32 [4, 8], P('view'), may hold values from 0 to 63
- pattern_shift: int32 [4, 8], P('view'), may hold values from 0 to 127
- interp: float32 [4, 8, 128], P('view'), may hold values from 0.05 to 0.45
Outputs:
- updated: float32 [4, 1024, 1024], P(None, 'slab')
Inputs may be any that keep to these rules, and one draw needn't show every extreme that they name: `psf`: every entry is positive.
All inputs are finite; a program needn't handle non-finite values.
Results may differ from a plain program's by a relative error of at most 0.0001.
Values sent between devices are 32-bit elements; how exact they have to be, the bound alone decides.
No kernel may reach another device: no remote copies, remote signals or barrier semaphores. Data moves between devices by JAX's collectives and lax.ppermute only.
A program may use at most 128 MiB of HBM per device.

v0:
```python
import math

import jax
import jax.numpy as jnp
from jax import lax
from jax.sharding import PartitionSpec as P

highest = lax.Precision.HIGHEST


def block_matrix(multiplier, shifting, weights):
    positions = jnp.arange(128, dtype=jnp.int32)
    first_col = ((2 * multiplier[:, None] + 1) * positions[None, :] + shifting[:, None]) % 128
    second_col = (first_col + 1) % 128
    columns = positions[None, None, :]
    lower = (columns == first_col[:, :, None]).astype(jnp.float32)
    upper = (columns == second_col[:, :, None]).astype(jnp.float32)
    return (1.0 - weights)[:, :, None] * lower + weights[:, :, None] * upper


def angle_tables(rows, cols, length):
    row_index = lax.iota(jnp.int32, rows)[:, None]
    col_index = lax.iota(jnp.int32, cols)[None, :]
    angles = (row_index * col_index % length).astype(jnp.float32) * (2.0 * math.pi / length)
    return (jnp.cos(angles), jnp.sin(angles))


def unit_root(numerator, length):
    angle = 2.0 * math.pi * numerator / length
    return (round(math.cos(angle), 15), round(math.sin(angle), 15))


def small_stage(real_part, imag_part, axis, direction):
    count = real_part.shape[axis]

    def part(array, index):
        return lax.index_in_dim(array, index, axis, keepdims=False)

    real_in = [part(real_part, index) for index in range(count)]
    imag_in = None if imag_part is None else [part(imag_part, index) for index in range(count)]
    real_out, imag_out = [], []
    for out_index in range(count):
        real_sum, imag_sum = None, None
        for in_index in range(count):
            cosine, sine = unit_root(in_index * out_index, count)
            sine = direction * sine
            terms_real = []
            terms_imag = []
            if cosine != 0.0:
                terms_real.append(cosine * real_in[in_index])
                if imag_in is not None:
                    terms_imag.append(cosine * imag_in[in_index])
            if sine != 0.0:
                terms_imag.append(sine * real_in[in_index])
                if imag_in is not None:
                    terms_real.append(-sine * imag_in[in_index])
            for term in terms_real:
                real_sum = term if real_sum is None else real_sum + term
            for term in terms_imag:
                imag_sum = term if imag_sum is None else imag_sum + term
        if imag_sum is None:
            imag_sum = jnp.zeros_like(real_sum)
        real_out.append(real_sum)
        imag_out.append(imag_sum)
    return (jnp.stack(real_out, axis), jnp.stack(imag_out, axis))


def complex_times(real_part, imag_part, cosine, sine_table):
    return (
        real_part * cosine - imag_part * sine_table,
        real_part * sine_table + imag_part * cosine,
    )


def block_dft_matrix(length, direction):
    cosine, sine = angle_tables(length, length, length)
    sine = direction * sine
    top = jnp.concatenate([cosine, sine], 1)
    bottom = jnp.concatenate([-sine, cosine], 1)
    return jnp.concatenate([top, bottom], 0)


def large_stage(real_part, imag_part, axis, direction):
    length = real_part.shape[axis]
    if imag_part is None:
        imag_part = jnp.zeros_like(real_part)
    joined = jnp.concatenate([real_part, imag_part], axis)
    matrix = block_dft_matrix(length, direction)
    if axis == joined.ndim - 1:
        out = jnp.einsum("...j,jn->...n", joined, matrix, precision=highest)
    else:
        out = jnp.einsum("rkjz,jn->rknz", joined, matrix, precision=highest)
    return (
        lax.slice_in_dim(out, 0, length, axis=axis),
        lax.slice_in_dim(out, length, 2 * length, axis=axis),
    )


def factored(real_part, imag_part, axis, direction, forward, want_imag=True):
    length = real_part.shape[axis]
    second = 128
    first = length // second
    outer = real_part.shape
    shape = outer[:axis] + (first, second) + outer[axis + 1 :]
    real_part = real_part.reshape(shape)
    if imag_part is not None:
        imag_part = imag_part.reshape(shape)
    twist_cos, twist_sin = angle_tables(first, second, length)
    if axis == 1:
        twist_cos = twist_cos[:, :, None]
        twist_sin = twist_sin[:, :, None]
    twist_sin = direction * twist_sin
    if forward:
        real_part, imag_part = small_stage(real_part, imag_part, axis, direction)
        real_part, imag_part = complex_times(real_part, imag_part, twist_cos, twist_sin)
        real_part, imag_part = large_stage(real_part, imag_part, axis + 1, direction)
    else:
        real_part, imag_part = large_stage(real_part, imag_part, axis + 1, direction)
        real_part, imag_part = complex_times(real_part, imag_part, twist_cos, twist_sin)
        real_part, imag_part = small_stage(real_part, imag_part, axis, direction)
    return (real_part.reshape(outer), imag_part.reshape(outer))


def to_columns(real_part, imag_part):
    depth_real, depth_imag = factored(real_part, imag_part, 2, -1.0, True)
    rows = depth_real.shape[0]
    stacked = jnp.concatenate([depth_real, depth_imag], 0)
    moved = lax.all_to_all(stacked, "slab", split_axis=2, concat_axis=1, tiled=True)
    return factored(moved[:rows], moved[rows:], 1, -1.0, True)


def to_planes(real_part, imag_part):
    width_real, width_imag = factored(real_part, imag_part, 1, 1.0, False)
    rows = width_real.shape[0]
    stacked = jnp.concatenate([width_real, width_imag], 0)
    moved = lax.all_to_all(stacked, "slab", split_axis=1, concat_axis=2, tiled=True)
    return factored(moved[:rows], moved[rows:], 2, 1.0, False)


def pack_pairs(volume):
    return (volume[0::2], volume[1::2])


def unpack_pairs(real_part, imag_part):
    pairs, width, depth = real_part.shape
    return jnp.stack([real_part, imag_part], 1).reshape(2 * pairs, width, depth)


def general_shards(estimate, views, psf, pattern_mult, pattern_shift, interp):
    row_count, slab_width, depth = estimate.shape
    blocks = block_matrix(pattern_mult[0], pattern_shift[0], interp[0])
    block_count = depth // 128
    shaped = estimate.reshape(row_count, slab_width, block_count, 128)
    sampled = jnp.einsum("bij,yxbj->yxbi", blocks, shaped, precision=highest).reshape(
        row_count, slab_width, depth
    )
    packed_real, packed_imag = pack_pairs(sampled)
    packed_real = jnp.concatenate([packed_real, psf], 0)
    packed_imag = jnp.concatenate([packed_imag, jnp.zeros_like(psf)], 0)
    spectra_real, spectra_imag = to_columns(packed_real, packed_imag)
    scaling = 1.0 / (spectra_real.shape[1] * depth)
    transfer_real = spectra_real[-1:] * scaling
    transfer_imag = spectra_imag[-1:] * scaling
    spectra_real = spectra_real[:-1]
    spectra_imag = spectra_imag[:-1]
    filtered_real = spectra_real * transfer_real - spectra_imag * transfer_imag
    filtered_imag = spectra_real * transfer_imag + spectra_imag * transfer_real
    blurred = unpack_pairs(*to_planes(filtered_real, filtered_imag))
    quotient = views[0] / blurred
    packed_real, packed_imag = pack_pairs(quotient)
    spectra_real, spectra_imag = to_columns(packed_real, packed_imag)
    filtered_real = spectra_real * transfer_real + spectra_imag * transfer_imag
    filtered_imag = spectra_imag * transfer_real - spectra_real * transfer_imag
    smeared = unpack_pairs(*to_planes(filtered_real, filtered_imag))
    correction = jnp.einsum(
        "bij,yxbi->yxbj",
        blocks,
        smeared.reshape(row_count, slab_width, block_count, 128),
        precision=highest,
    ).reshape(row_count, slab_width, depth)
    log_terms = jnp.log(correction)
    view_count = lax.axis_size("view")
    summed = lax.psum(log_terms, "view")
    return estimate * jnp.exp(summed / view_count)


def swap_halves(joined):
    half = joined.shape[-1] // 2
    return jnp.concatenate([-joined[..., half:], joined[..., :half]], -1)


def butterflies(parts, direction, turn):
    count = len(parts)
    if count == 1:
        return parts
    even = butterflies(parts[0::2], direction, turn)
    odd = butterflies(parts[1::2], direction, turn)
    out = [None] * count
    for index in range(count // 2):
        cosine, sine = unit_root(index, count)
        sine = direction * sine
        value = odd[index]
        if sine == 0.0:
            rotated = value if cosine > 0 else -value
        elif cosine == 0.0:
            rotated = turn(value) if sine > 0 else -turn(value)
        else:
            rotated = cosine * value + sine * turn(value)
        out[index] = even[index] + rotated
        out[index + count // 2] = even[index] - rotated
    return out


def lead_stage(joined, direction):
    count = joined.shape[0]
    parts = [joined[index] for index in range(count)]
    return jnp.stack(butterflies(parts, direction, swap_halves), 0)


def joined_twist(joined, length, direction, lanes):
    first, second = joined.shape[0], (joined.shape[-1] // 2 if lanes else joined.shape[2])
    cosine, sine = angle_tables(first, second, length)
    sine = direction * sine
    if lanes:
        cosine = jnp.concatenate([cosine, cosine], 1)[:, None, None, :]
        sine = jnp.concatenate([sine, sine], 1)[:, None, None, :]
    else:
        cosine = cosine[:, None, :, None]
        sine = sine[:, None, :, None]
    return joined * cosine + swap_halves(joined) * sine


def lane_stage(joined, direction):
    length = joined.shape[-1] // 2
    matrix = block_dft_matrix(length, direction)
    return jnp.einsum("...j,jn->...n", joined, matrix, precision=lax.Precision.HIGH)


def row_stage(joined, direction):
    length = joined.shape[2]
    cosine, sine = angle_tables(length, length, length)
    matrix = jnp.concatenate([cosine, direction * sine], 0)
    both = jnp.concatenate([joined, swap_halves(joined)], 2)
    return jnp.einsum("krjl,jm->krml", both, matrix, precision=lax.Precision.HIGH)


def depth_forward(joined, depth):
    joined = lead_stage(joined, -1.0)
    joined = joined_twist(joined, depth, -1.0, True)
    return lane_stage(joined, -1.0)


def depth_inverse(joined, depth):
    joined = lane_stage(joined, 1.0)
    joined = joined_twist(joined, depth, 1.0, True)
    return lead_stage(joined, 1.0)


def width_forward(joined, width):
    joined = lead_stage(joined, -1.0)
    joined = joined_twist(joined, width, -1.0, False)
    return row_stage(joined, -1.0)


def width_inverse(joined, width):
    joined = row_stage(joined, 1.0)
    joined = joined_twist(joined, width, 1.0, False)
    return lead_stage(joined, 1.0)


def joined_times(joined, transfer_real, transfer_imag):
    return joined * transfer_real + swap_halves(joined) * transfer_imag


def to_blocks(volume, block_count):
    rows, width, depth = volume.shape
    lanes = depth // block_count
    parity = [volume[0::2], volume[1::2]]
    return jnp.stack(
        [
            jnp.concatenate([part[:, :, block * lanes : (block + 1) * lanes] for part in parity], -1)
            for block in range(block_count)
        ],
        0,
    )


def from_blocks(blocked):
    block_count, pairs, width, lanes = blocked.shape
    half = lanes // 2
    parity = [
        jnp.concatenate([blocked[block, :, :, side * half : (side + 1) * half] for block in range(block_count)], -1)
        for side in range(2)
    ]
    return jnp.stack(parity, 1).reshape(2 * pairs, width, block_count * half)


def shards(estimate, views, psf, pattern_mult, pattern_shift, interp):
    row_count, slab_width, depth = estimate.shape
    slab_count = lax.axis_size("slab")
    block_count = depth // 128
    width = slab_width * slab_count
    if not (
        block_count == slab_count
        and slab_width == 128
        and width // 128 == slab_count
        and row_count % 2 == 0
    ):
        return general_shards(estimate, views, psf, pattern_mult, pattern_shift, interp)
    blocks = block_matrix(pattern_mult[0], pattern_shift[0], interp[0])
    empty = jnp.zeros_like(blocks)
    doubled = jnp.concatenate(
        [jnp.concatenate([blocks, empty], 2), jnp.concatenate([empty, blocks], 2)], 1
    )
    sampled = jnp.einsum(
        "apxl,aml->apxm", to_blocks(estimate, block_count), doubled, precision=lax.Precision.HIGH
    )
    pairs = row_count // 2
    spread = psf.reshape(slab_width, block_count, 128).transpose(1, 0, 2)[:, None]
    spread = jnp.concatenate([spread, jnp.zeros_like(spread)], -1)
    def to_columns_blocked(planes):
        spectra = depth_forward(planes, depth)
        spectra = lax.all_to_all(spectra, "slab", split_axis=0, concat_axis=0, tiled=True)
        return width_forward(spectra, width)

    transfer = to_columns_blocked(spread) * (1.0 / (width * depth))
    spectra = to_columns_blocked(sampled)
    half = transfer.shape[-1] // 2
    transfer_real = jnp.concatenate([transfer[..., :half], transfer[..., :half]], -1)
    transfer_imag = jnp.concatenate([transfer[..., half:], transfer[..., half:]], -1)

    def convolve(spectra, transfer_imag):
        filtered = joined_times(spectra, transfer_real, transfer_imag)
        planes = width_inverse(filtered, width)
        planes = lax.all_to_all(planes, "slab", split_axis=0, concat_axis=0, tiled=True)
        return depth_inverse(planes, depth)

    blurred = convolve(spectra, transfer_imag)
    quotient = to_blocks(views[0], block_count) / blurred
    spectra = depth_forward(quotient, depth)
    spectra = lax.all_to_all(spectra, "slab", split_axis=0, concat_axis=0, tiled=True)
    spectra = width_forward(spectra, width)
    smeared = convolve(spectra, -transfer_imag)
    correction = jnp.einsum("apxm,aml->apxl", smeared, doubled, precision=lax.Precision.HIGH)
    log_terms = from_blocks(jnp.log(correction))
    view_count = lax.axis_size("view")
    summed = lax.psum(log_terms, "view")
    return estimate * jnp.exp(summed / view_count)


def solution(mesh):
    placed = (
        P(None, "slab", None),
        P("view", None, "slab", None),
        P("view", "slab", None),
        P("view", None),
        P("view", None),
        P("view", None, None),
    )
    return jax.shard_map(
        shards, mesh=mesh, in_specs=placed, out_specs=P(None, "slab", None), check_vma=False
    )
```

profile of v0, /device:TPU:0, one launch (start us, length us, event | category | flops | bytes accessed | tf_op | source)
XLA Modules:
  0.0 285.5 jit_solution(3338076680275577387)
XLA Ops:
  7.2 1.2 copy.41
  9.5 1.6 convolution_bitcast_fusion
  11.1 5.2 %all-to-all-start.1 = ((f32[8,1,128,256]{3,2,1,0:T(8,128)}), f32[8,1,128,256]{3,2,1,0:T(8,128)S(1)}, u32[]{:S(2)}, u32[]{:S(2)}) async-start(f32[8,1,128,256]{3,2,1,0:T(8,128)} %convolution_bitcast_fusion), calls=%async_computation.1 | async-start | bytes 2097152 | tf_op jit(solution)/shard_map/all_to_all | solution.py:323
  18.8 1.1 fusion.52
  21.4 2.4 fusion.26
  23.8 7.9 %all-to-all-done.1 = f32[8,1,128,256]{3,2,1,0:T(8,128)S(1)} async-done(((f32[8,1,128,256]{3,2,1,0:T(8,128)}), f32[8,1,128,256]{3,2,1,0:T(8,128)S(1)}, u32[]{:S(2)}, u32[]{:S(2)}) %all-to-all-start.1) | async-done | bytes 1048608 | tf_op jit(solution)/shard_map/all_to_all | solution.py:323
  31.7 3.8 %all-to-all-start = ((f32[8,2,128,256]{3,2,1,0:T(8,128)}), f32[8,2,128,256]{3,2,1,0:T(8,128)S(1)}, u32[]{:S(2)}, u32[]{:S(2)}) async-start(f32[8,2,128,256]{3,2,1,0:T(8,128)} %fusion.26), calls=%async_computation | async-start | bytes 4194304 | tf_op jit(solution)/shard_map/all_to_all | solution.py:323
  37.6 1.0 slice_bitcast_fusion.67
  38.6 1.0 maximum_bitcast_fusion.7
  39.7 22.2 %all-to-all-done = f32[8,2,128,256]{3,2,1,0:T(8,128)S(1)} async-done(((f32[8,2,128,256]{3,2,1,0:T(8,128)}), f32[8,2,128,256]{3,2,1,0:T(8,128)S(1)}, u32[]{:S(2)}, u32[]{:S(2)}) %all-to-all-start) | async-done | bytes 2097184 | tf_op jit(solution)/shard_map/all_to_all | solution.py:323
  63.8 1.6 fusion.66
  65.7 1.0 copy-done.3
  67.3 1.5 fusion.63
  69.4 0.9 subtract_bitcast_fusion.15
  76.1 3.8 %all-to-all-start.2 = ((f32[8,2,128,256]{3,2,1,0:T(8,128)}), f32[8,2,128,256]{3,2,1,0:T(8,128)S(1)}, u32[]{:S(2)}, u32[]{:S(2)}) async-start(f32[8,2,128,256]{3,2,1,0:T(8,128)} %subtract_dynamic-update-slice_fusion.20), calls=%async_computation.2 | async-start | bytes 4194304 | tf_op jit(solution)/shard_map/all_to_all | solution.py:335
  80.2 1.7 fusion.269
  88.0 18.4 %all-to-all-done.2 = f32[8,2,128,256]{3,2,1,0:T(8,128)S(1)} async-done(((f32[8,2,128,256]{3,2,1,0:T(8,128)}), f32[8,2,128,256]{3,2,1,0:T(8,128)S(1)}, u32[]{:S(2)}, u32[]{:S(2)}) %all-to-all-start.2) | async-done | bytes 2097184 | tf_op jit(solution)/shard_map/all_to_all | solution.py:335
  106.3 1.0 fusion.128
  109.0 2.0 div.9
  112.4 2.4 fusion.40
  114.8 3.6 %all-to-all-start.3 = ((f32[8,2,128,256]{3,2,1,0:T(8,128)}), f32[8,2,128,256]{3,2,1,0:T(8,128)S(1)}, u32[]{:S(2)}, u32[]{:S(2)}) async-start(f32[8,2,128,256]{3,2,1,0:T(8,128)} %fusion.40), calls=%async_computation.3 | async-start | bytes 4194304 | tf_op jit(solution)/shard_map/all_to_all | solution.py:341
  118.7 2.2 maximum_negate_fusion
  121.0 24.0 %all-to-all-done.3 = f32[8,2,128,256]{3,2,1,0:T(8,128)S(1)} async-done(((f32[8,2,128,256]{3,2,1,0:T(8,128)}), f32[8,2,128,256]{3,2,1,0:T(8,128)S(1)}, u32[]{:S(2)}, u32[]{:S(2)}) %all-to-all-start.3) | async-done | bytes 2097184 | tf_op jit(solution)/shard_map/all_to_all | solution.py:341
  147.0 1.6 fusion.60
  148.8 1.0 copy-done.2
  150.4 1.5 fusion.57
  153.7 29.0 %all_to_all.25 = f32[8,2,128,256]{3,2,1,0:T(8,128)S(1)} all-to-all(f32[8,2,128,256]{3,2,1,0:T(8,128)S(1)} %subtract_dynamic-update-slice_fusion.4), channel_id=1, replica_groups=mesh['slab'=8,'view'=4] {'slab'}, dimensions={0} | all-to-all | bytes 4194304 | tf_op jit(solution)/shard_map/all_to_all | solution.py:335
  182.8 1.0 fusion.126
  186.3 1.1 fusion.54
  187.9 1.5 copy.69
  189.3 86.0 %all-reduce.5.cloned.1.call-done = f32[4,128,1024]{2,1,0:T(8,128)} async-done(((f32[4,128,1024]{2,1,0:T(8,128)}), f32[4,128,1024]{2,1,0:T(8,128)}) %all-reduce.5.cloned.1.call-update) | async-done | bytes 2097168 | tf_op jit(solution)/shard_map/psum | solution.py:347
  275.4 3.3 %exponential_multiply_fusion = f32[4,128,1024]{2,1,0:T(8,128)} fusion(f32[4,128,1024]{2,1,0:T(8,128)S(1)} %copy-done.1, f32[4,128,1024]{2,1,0:T(8,128)} %all-reduce.5.cloned.1.call-done), kind=kLoop, calls=%fused_computation.69 | loop fusion | flops 1048576 | bytes 6291456 | tf_op jit(solution)/shard_map/mul | solution.py:348
  (245 shorter events, 33.3 us)
Async XLA Ops:
  9.5 7.0 %copy-start = (f32[4,128,1024]{2,1,0:T(8,128)S(1)}, f32[4,128,1024]{2,1,0:T(8,128)}, u32[]{:S(2)}) copy-start(f32[4,128,1024]{2,1,0:T(8,128)} %param.6) | copy-start | bytes 6291460
  11.1 20.6 %all-to-all-start.1 = ((f32[8,1,128,256]{3,2,1,0:T(8,128)}), f32[8,1,128,256]{3,2,1,0:T(8,128)S(1)}, u32[]{:S(2)}, u32[]{:S(2)}) async-start(f32[8,1,128,256]{3,2,1,0:T(8,128)} %convolution_bitcast_fusion), calls=%async_computation.1 | async-start | bytes 2097152 | tf_op jit(solution)/shard_map/all_to_all | solution.py:323
  16.5 0.7 copy-start.8
  16.6 0.7 copy-start.6
  17.3 0.7 copy-start.7
  18.8 1.1 copy-start.4
  31.7 30.2 %all-to-all-start = ((f32[8,2,128,256]{3,2,1,0:T(8,128)}), f32[8,2,128,256]{3,2,1,0:T(8,128)S(1)}, u32[]{:S(2)}, u32[]{:S(2)}) async-start(f32[8,2,128,256]{3,2,1,0:T(8,128)} %fusion.26), calls=%async_computation | async-start | bytes 4194304 | tf_op jit(solution)/shard_map/all_to_all | solution.py:323
  65.4 1.2 copy-start.3
  76.1 30.2 %all-to-all-start.2 = ((f32[8,2,128,256]{3,2,1,0:T(8,128)}), f32[8,2,128,256]{3,2,1,0:T(8,128)S(1)}, u32[]{:S(2)}, u32[]{:S(2)}) async-start(f32[8,2,128,256]{3,2,1,0:T(8,128)} %subtract_dynamic-update-slice_fusion.20), calls=%async_computation.2 | async-start | bytes 4194304 | tf_op jit(solution)/shard_map/all_to_all | solution.py:335
  114.8 30.2 %all-to-all-start.3 = ((f32[8,2,128,256]{3,2,1,0:T(8,128)}), f32[8,2,128,256]{3,2,1,0:T(8,128)S(1)}, u32[]{:S(2)}, u32[]{:S(2)}) async-start(f32[8,2,128,256]{3,2,1,0:T(8,128)} %fusion.40), calls=%async_computation.3 | async-start | bytes 4194304 | tf_op jit(solution)/shard_map/all_to_all | solution.py:341
  118.4 156.9 %all-reduce.5.cloned.1.call-start = ((), (), s32[]{:S(2)}) async-start(), calls=%async_computation.5 | async-start | bytes 4194304 | tf_op jit(solution)/shard_map/psum | solution.py:347
  148.5 1.2 copy-start.2
  185.2 1.0 copy-start.5
  189.3 86.0 %copy-start.1 = (f32[4,128,1024]{2,1,0:T(8,128)S(1)}, f32[4,128,1024]{2,1,0:T(8,128)}, u32[]{:S(2)}) copy-start(f32[4,128,1024]{2,1,0:T(8,128)} %param.6) | copy-start | bytes 6291460
Sparse Core Ops, SparseCore 0:
  189.5 85.8 all-reduce.4
where the time goes:
time: 286 us
  waiting for transfers between devices  158 us (55%)
  other arithmetic  38.9 us (14%)
  blocking collectives  29 us (10%)
  matrix products  17.6 us (6%)
  starting transfers between devices  16.7 us (6%)
  between operations  14.8 us (5%)
  local copies, waits for them, and re-layouts  9.96 us (3%)
    psum x1, waiting for transfers between devices, shards(): summed = lax.psum(log_terms, 'view')  86 us
    all_to_all x2, waiting for transfers between devices, to_columns_blocked(): lax.all_to_all(spectra, 'slab', split_axis=0, concat_axis=0, tiled=True)  30.1 us
    all_to_all x1, blocking collectives, convolve(): lax.all_to_all(planes, 'slab', split_axis=0, concat_axis=0, tiled=True)  29 us
    all_to_all x1, waiting for transfers between devices, shards(): lax.all_to_all(spectra, 'slab', split_axis=0, concat_axis=0, tiled=True)  24 us
    all_to_all x1, waiting for transfers between devices, convolve(): lax.all_to_all(planes, 'slab', split_axis=0, concat_axis=0, tiled=True)  18.4 us
    unnamed x82, other arithmetic  14.6 us
    all_to_all x2, starting transfers between devices, to_columns_blocked(): lax.all_to_all(spectra, 'slab', split_axis=0, concat_axis=0, tiled=True)  8.95 us
    dot_general x5, matrix products, lane_stage(): jnp.einsum('...j,jn->...n', joined, matrix, precision=lax.Precision.HIGH)  8.46 us
  transfers between devices with their start and end apart: 5, of which 5 were waited for; matrix products, arithmetic and copies ran while one was open for 7% of the time, Pallas kernels for 0%

commit v1 on v0

--- a/solution.py
+++ b/solution.py
@@ -244,27 +244,75 @@
     return jnp.einsum("krjl,jm->krml", both, matrix, precision=lax.Precision.HIGH)
 
 
+def twist_parts(count, length, size, direction):
+    cosine, sine = angle_tables(count, size, length)
+    return cosine, direction * sine
+
+
+def depth_matrices(count, length, direction, twist_first):
+    half = length // count
+    matrix = block_dft_matrix(half, direction)
+    cosine, sine = twist_parts(count, length, half, direction)
+    top, bottom = matrix[:half], matrix[half:]
+    left, right = matrix[:, :half], matrix[:, half:]
+    if twist_first:
+        return jnp.concatenate(
+            [
+                cosine[:, :, None] * top + sine[:, :, None] * bottom,
+                -sine[:, :, None] * top + cosine[:, :, None] * bottom,
+            ],
+            1,
+        )
+    return jnp.concatenate(
+        [
+            left * cosine[:, None, :] - right * sine[:, None, :],
+            left * sine[:, None, :] + right * cosine[:, None, :],
+        ],
+        2,
+    )
+
+
+def width_matrices(count, length, direction, twist_first):
+    half = length // count
+    cosine_table, sine_table = angle_tables(half, half, half)
+    sine_table = direction * sine_table
+    cosine, sine = twist_parts(count, length, half, direction)
+    if twist_first:
+        c, s = cosine[:, :, None], sine[:, :, None]
+    else:
+        c, s = cosine[:, None, :], sine[:, None, :]
+    if twist_first:
+        return jnp.concatenate(
+            [cosine_table * c - sine_table * s, cosine_table * s + sine_table * c], 1
+        )
+    return jnp.concatenate(
+        [cosine_table * c - sine_table * s, sine_table * c + cosine_table * s], 1
+    )
+
+
 def depth_forward(joined, depth):
     joined = lead_stage(joined, -1.0)
-    joined = joined_twist(joined, depth, -1.0, True)
-    return lane_stage(joined, -1.0)
+    matrices = depth_matrices(joined.shape[0], depth, -1.0, True)
+    return jnp.einsum("krxj,kjn->krxn", joined, matrices, precision=lax.Precision.HIGH)
 
 
 def depth_inverse(joined, depth):
-    joined = lane_stage(joined, 1.0)
-    joined = joined_twist(joined, depth, 1.0, True)
+    matrices = depth_matrices(joined.shape[0], depth, 1.0, False)
+    joined = jnp.einsum("krxj,kjn->krxn", joined, matrices, precision=lax.Precision.HIGH)
     return lead_stage(joined, 1.0)
 
 
 def width_forward(joined, width):
     joined = lead_stage(joined, -1.0)
-    joined = joined_twist(joined, width, -1.0, False)
-    return row_stage(joined, -1.0)
+    matrices = width_matrices(joined.shape[0], width, -1.0, True)
+    both = jnp.concatenate([joined, swap_halves(joined)], 2)
+    return jnp.einsum("krjl,kjm->krml", both, matrices, precision=lax.Precision.HIGH)
 
 
 def width_inverse(joined, width):
-    joined = row_stage(joined, 1.0)
-    joined = joined_twist(joined, width, 1.0, False)
+    matrices = width_matrices(joined.shape[0], width, 1.0, False)
+    both = jnp.concatenate([joined, swap_halves(joined)], 2)
+    joined = jnp.einsum("krjl,kjm->krml", both, matrices, precision=lax.Precision.HIGH)
     return lead_stage(joined, 1.0)
 
 

time: 286 us -> 292 us (1.021)
  local copies, waits for them, and re-layouts: 9.96 us -> 22.6 us
  other arithmetic: 38.9 us -> 29.2 us
  matrix products: 17.6 us -> 20.9 us
    unnamed x26 -> x74, local copies, waits for them, and re-layouts: 4.88 us -> 16.1 us
    all_to_all x2, waiting for transfers between devices: 30.1 us -> 22.4 us  [to_columns_blocked(): lax.all_to_all(spectra, 'slab', split_axis=0, concat_axis=0, tiled=True)]
    all_to_all x1, waiting for transfers between devices: 18.4 us -> 24.5 us  [convolve(): lax.all_to_all(planes, 'slab', split_axis=0, concat_axis=0, tiled=True)]
    unnamed x82 -> x76, other arithmetic: 14.6 us -> 9.75 us
    dot_general x10, matrix products: 15.4 us -> 18.7 us  [the longest x3 6.96 us: depth_forward(): jnp.einsum('krxj,kjn->krxn', joined, matrices, precision=lax.Precision.HIGH)]
  transfers between devices with their start and end apart: 5 -> 5, of which waited for: 5 -> 5; matrix products, arithmetic and copies ran while one was open for 7% -> 6% of each run, Pallas kernels for 0% -> 0%
where the time goes in v1:
time: 292 us; the launch traced here: 291 us
  waiting for transfers between devices  157 us (54%)
  other arithmetic  29.2 us (10%)
  blocking collectives  29.2 us (10%)
  local copies, waits for them, and re-layouts  22.6 us (8%)
  matrix products  20.9 us (7%)
  starting transfers between devices  17.3 us (6%)
  between operations  15 us (5%)
    psum x1, waiting for transfers between devices, shards(): summed = lax.psum(log_terms, 'view')  86 us
    all_to_all x1, blocking collectives, convolve(): lax.all_to_all(planes, 'slab', split_axis=0, concat_axis=0, tiled=True)  29.2 us
    all_to_all x1, waiting for transfers between devices, convolve(): lax.all_to_all(planes, 'slab', split_axis=0, concat_axis=0, tiled=True)  24.5 us
    all_to_all x1, waiting for transfers between devices, shards(): lax.all_to_all(spectra, 'slab', split_axis=0, concat_axis=0, tiled=True)  24.1 us
    all_to_all x2, waiting for transfers between devices, to_columns_blocked(): lax.all_to_all(spectra, 'slab', split_axis=0, concat_axis=0, tiled=True)  22.4 us
    unnamed x74, local copies, waits for them, and re-layouts  16.1 us
    unnamed x76, other arithmetic  9.75 us
    all_to_all x2, starting transfers between devices, to_columns_blocked(): lax.all_to_all(spectra, 'slab', split_axis=0, concat_axis=0, tiled=True)  8.96 us
  transfers between devices with their start and end apart: 5, of which 5 were waited for; matrix products, arithmetic and copies ran while one was open for 6% of the time, Pallas kernels for 0%

profile of v1, /device:TPU:0, one launch (start us, length us, event | category | flops | bytes accessed | tf_op | source)
XLA Modules:
  0.0 291.2 jit_solution(13636733864450008579)
XLA Ops:
  6.5 1.2 copy.35
  9.7 1.9 convolution_bitcast_fusion
  11.6 5.2 %all-to-all-start.1 = ((f32[8,1,128,256]{3,2,1,0:T(8,128)}), f32[8,1,128,256]{3,2,1,0:T(8,128)S(1)}, u32[]{:S(2)}, u32[]{:S(2)}) async-start(f32[8,1,128,256]{3,2,1,0:T(8,128)} %convolution_bitcast_fusion), calls=%async_computation.1 | async-start | bytes 2097152 | tf_op jit(solution)/shard_map/all_to_all | solution.py:371
  17.0 1.7 fusion.226
  20.3 1.1 fusion.38
  22.6 1.3 copy-done.23
  24.3 1.7 multiply_subtract_fusion.2
  26.5 1.5 fusion.227
  28.9 2.5 fusion.34
  32.2 3.8 %all-to-all-start = ((f32[8,2,128,256]{3,2,1,0:T(8,128)}), f32[8,2,128,256]{3,2,1,0:T(8,128)S(1)}, u32[]{:S(2)}, u32[]{:S(2)}) async-start(f32[8,2,128,256]{3,2,1,0:T(8,128)} %fusion.34), calls=%async_computation | async-start | bytes 4194304 | tf_op jit(solution)/shard_map/all_to_all | solution.py:371
  38.6 1.0 slice_bitcast_fusion.67
  39.6 1.1 maximum_bitcast_fusion.11
  40.8 21.6 %all-to-all-done = f32[8,2,128,256]{3,2,1,0:T(8,128)S(1)} async-done(((f32[8,2,128,256]{3,2,1,0:T(8,128)}), f32[8,2,128,256]{3,2,1,0:T(8,128)S(1)}, u32[]{:S(2)}, u32[]{:S(2)}) %all-to-all-start) | async-done | bytes 2097184 | tf_op jit(solution)/shard_map/all_to_all | solution.py:371
  64.6 1.7 fusion.54
  69.2 1.6 fusion.51
  77.7 4.5 %all-to-all-start.2 = ((f32[8,2,128,256]{3,2,1,0:T(8,128)}), f32[8,2,128,256]{3,2,1,0:T(8,128)}, u32[]{:S(2)}, u32[]{:S(2)}) async-start(f32[8,2,128,256]{3,2,1,0:T(8,128)} %subtract_dynamic-update-slice_fusion.20), calls=%async_computation.2 | async-start | bytes 4194304 | tf_op jit(solution)/shard_map/all_to_all | solution.py:383
  82.7 1.3 copy-done.25
  84.3 24.5 %all-to-all-done.2 = f32[8,2,128,256]{3,2,1,0:T(8,128)} async-done(((f32[8,2,128,256]{3,2,1,0:T(8,128)}), f32[8,2,128,256]{3,2,1,0:T(8,128)}, u32[]{:S(2)}, u32[]{:S(2)}) %all-to-all-start.2) | async-done | bytes 2097184 | tf_op jit(solution)/shard_map/all_to_all | solution.py:383
  108.8 2.8 fusion.41
  112.8 1.3 copy-done.26
  116.7 2.6 fusion.32
  119.3 3.6 %all-to-all-start.3 = ((f32[8,2,128,256]{3,2,1,0:T(8,128)}), f32[8,2,128,256]{3,2,1,0:T(8,128)S(1)}, u32[]{:S(2)}, u32[]{:S(2)}) async-start(f32[8,2,128,256]{3,2,1,0:T(8,128)} %fusion.32), calls=%async_computation.3 | async-start | bytes 4194304 | tf_op jit(solution)/shard_map/all_to_all | solution.py:389
  123.2 2.2 maximum_negate_fusion
  125.4 24.1 %all-to-all-done.3 = f32[8,2,128,256]{3,2,1,0:T(8,128)S(1)} async-done(((f32[8,2,128,256]{3,2,1,0:T(8,128)}), f32[8,2,128,256]{3,2,1,0:T(8,128)S(1)}, u32[]{:S(2)}, u32[]{:S(2)}) %all-to-all-start.3) | async-done | bytes 2097184 | tf_op jit(solution)/shard_map/all_to_all | solution.py:389
  151.8 1.7 fusion.48
  156.6 1.7 fusion.45
  159.5 29.2 %all_to_all.25 = f32[8,2,128,256]{3,2,1,0:T(8,128)S(1)} all-to-all(f32[8,2,128,256]{3,2,1,0:T(8,128)S(1)} %subtract_dynamic-update-slice_fusion.4), channel_id=1, replica_groups=mesh['slab'=8,'view'=4] {'slab'}, dimensions={0} | all-to-all | bytes 4194304 | tf_op jit(solution)/shard_map/all_to_all | solution.py:383
  188.7 1.3 fusion.40
  191.9 1.1 fusion.42
  193.5 1.5 copy.59
  194.9 86.0 %all-reduce.5.cloned.1.call-done = f32[4,128,1024]{2,1,0:T(8,128)} async-done(((f32[4,128,1024]{2,1,0:T(8,128)}), f32[4,128,1024]{2,1,0:T(8,128)}) %all-reduce.5.cloned.1.call-update) | async-done | bytes 2097168 | tf_op jit(solution)/shard_map/psum | solution.py:395
  281.0 3.3 %exponential_multiply_fusion = f32[4,128,1024]{2,1,0:T(8,128)} fusion(f32[4,128,1024]{2,1,0:T(8,128)S(1)} %copy-done.14, f32[4,128,1024]{2,1,0:T(8,128)} %all-reduce.5.cloned.1.call-done), kind=kLoop, calls=%fused_computation.53 | loop fusion | flops 1048576 | bytes 6291456 | tf_op jit(solution)/shard_map/mul | solution.py:396
  (275 shorter events, 34.7 us)
Async XLA Ops:
  9.7 18.3 %copy-start = (f32[8,128,256]{2,1,0:T(8,128)}, f32[8,128,256]{2,1,0:T(8,128)S(1)}, u32[]{:S(2)}) copy-start(f32[8,128,256]{2,1,0:T(8,128)S(1)} %get-tuple-element.182) | copy-start | bytes 3145732
  9.7 18.3 %copy-start.2 = (f32[8,128,256]{2,1,0:T(8,128)}, f32[8,128,256]{2,1,0:T(8,128)S(1)}, u32[]{:S(2)}) copy-start(f32[8,128,256]{2,1,0:T(8,128)S(1)} %get-tuple-element.183) | copy-start | bytes 3145732
  11.6 20.6 %all-to-all-start.1 = ((f32[8,1,128,256]{3,2,1,0:T(8,128)}), f32[8,1,128,256]{3,2,1,0:T(8,128)S(1)}, u32[]{:S(2)}, u32[]{:S(2)}) async-start(f32[8,1,128,256]{3,2,1,0:T(8,128)} %convolution_bitcast_fusion), calls=%async_computation.1 | async-start | bytes 2097152 | tf_op jit(solution)/shard_map/all_to_all | solution.py:371
  17.0 1.7 copy-start.32
  17.0 1.7 copy-start.30
  20.3 1.1 copy-start.28
  22.6 1.3 copy-start.23
  24.3 2.2 copy-start.27
  26.5 2.3 copy-start.24
  32.2 30.2 %all-to-all-start = ((f32[8,2,128,256]{3,2,1,0:T(8,128)}), f32[8,2,128,256]{3,2,1,0:T(8,128)S(1)}, u32[]{:S(2)}, u32[]{:S(2)}) async-start(f32[8,2,128,256]{3,2,1,0:T(8,128)} %fusion.34), calls=%async_computation | async-start | bytes 4194304 | tf_op jit(solution)/shard_map/all_to_all | solution.py:371
  36.5 1.2 copy-start.11
  39.6 27.0 %copy-start.6 = (f32[8,128,256]{2,1,0:T(8,128)}, f32[8,128,256]{2,1,0:T(8,128)S(1)}, u32[]{:S(2)}) copy-start(f32[8,128,256]{2,1,0:T(8,128)S(1)} %maximum_bitcast_fusion.10) | copy-start | bytes 3145732
  63.4 1.0 copy-start.9
  63.4 1.2 copy-start.12
  66.4 1.2 copy-start.22
  68.0 1.2 copy-start.17
  77.7 4.5 %copy-start.19 = (f32[2,128,1024]{2,1,0:T(8,128)S(1)}, f32[2,128,1024]{2,1,0:T(8,128)}, u32[]{:S(2)}) copy-start(f32[2,128,1024]{2,1,0:T(8,128)} %get-tuple-element.135) | copy-start | bytes 3145732
  77.7 4.5 %copy-start.20 = (f32[2,128,1024]{2,1,0:T(8,128)S(1)}, f32[2,128,1024]{2,1,0:T(8,128)}, u32[]{:S(2)}) copy-start(f32[2,128,1024]{2,1,0:T(8,128)} %get-tuple-element.136) | copy-start | bytes 3145732
  77.7 31.1 %all-to-all-start.2 = ((f32[8,2,128,256]{3,2,1,0:T(8,128)}), f32[8,2,128,256]{3,2,1,0:T(8,128)}, u32[]{:S(2)}, u32[]{:S(2)}) async-start(f32[8,2,128,256]{3,2,1,0:T(8,128)} %subtract_dynamic-update-slice_fusion.20), calls=%async_computation.2 | async-start | bytes 4194304 | tf_op jit(solution)/shard_map/all_to_all | solution.py:383
  82.7 1.3 copy-start.25
  84.3 27.3 %copy-start.4 = (f32[8,256,128]{2,1,0:T(8,128)}, f32[8,256,128]{2,1,0:T(8,128)S(1)}, u32[]{:S(2)}) copy-start(f32[8,256,128]{2,1,0:T(8,128)S(1)} %get-tuple-element.181) | copy-start | bytes 3145732
  112.5 1.6 copy-start.26
  115.2 1.2 copy-start.1
  115.2 1.5 copy-start.3
  119.3 30.2 %all-to-all-start.3 = ((f32[8,2,128,256]{3,2,1,0:T(8,128)}), f32[8,2,128,256]{3,2,1,0:T(8,128)S(1)}, u32[]{:S(2)}, u32[]{:S(2)}) async-start(f32[8,2,128,256]{3,2,1,0:T(8,128)} %fusion.32), calls=%async_computation.3 | async-start | bytes 4194304 | tf_op jit(solution)/shard_map/all_to_all | solution.py:389
  122.9 158.1 %all-reduce.5.cloned.1.call-start = ((), (), s32[]{:S(2)}) async-start(), calls=%async_computation.5 | async-start | bytes 4194304 | tf_op jit(solution)/shard_map/psum | solution.py:395
  150.6 1.2 copy-start.13
  153.5 1.2 copy-start.7
  153.5 1.5 copy-start.21
  155.4 1.2 copy-start.18
  159.5 29.2 %copy-start.5 = (f32[8,256,128]{2,1,0:T(8,128)S(1)}, f32[8,256,128]{2,1,0:T(8,128)}, u32[]{:S(2)}) copy-start(f32[8,256,128]{2,1,0:T(8,128)} %copy-done.4) | copy-start | bytes 3145732
  194.9 86.1 %copy-start.14 = (f32[4,128,1024]{2,1,0:T(8,128)S(1)}, f32[4,128,1024]{2,1,0:T(8,128)}, u32[]{:S(2)}) copy-start(f32[4,128,1024]{2,1,0:T(8,128)} %param.6) | copy-start | bytes 6291460
  (6 other events, 5.9 us)
Sparse Core Ops, SparseCore 0:
  195.1 85.8 all-reduce.4
